TPU v7x, 256 devices: a whole 4x4x8 slice. The times are simulated.
256 devices in a mesh: seq: 64 (over y, z, core), tr: 2 (over x_lo), tc: 2 (over x_hi).
Axes of the slice: x: 4 (x_hi: 2, x_lo: 2; x = x_hi * 2 + x_lo), y: 4, z: 8, core: 2. Of those that a mesh axis runs over, the one named last changes fastest.
Arguments:
- activations: bfloat16 [65536, 1024], P('seq', ('tr', 'tc')), may hold values from -6 to 6
- seg_len: int32 [64], P('seq'), may hold values from 1 to 1024, as said below
- seg_start: int32 [64], P('seq'), may hold values from 0 to 1, as said below
- memory_rates: float32 [3, 64, 8], P(None, 'seq'), may hold values from 0 to 1, as said below
- w_qkv: bfloat16 [1024, 3, 1024], P(None, None, ('tr', 'tc')), may hold values from -0.1875 to 0.1875
- conv_w: float32 [4, 3, 1024], P(None, None, ('tr', 'tc')), may hold values from -3 to 3
- persistent: bfloat16 [2, 16, 1024], P(None, None, ('tr', 'tc')), may hold values from -6 to 6
- w_out: bfloat16 [1024, 1024], P(('tr', 'tc')), may hold values from -0.1875 to 0.1875
- w_gate: bfloat16 [1024, 2816], P(None, ('tr', 'tc')), may hold values from -0.1875 to 0.1875
- w_up: bfloat16 [1024, 2816], P(None, ('tr', 'tc')), may hold values from -0.1875 to 0.1875
- w_down: bfloat16 [2816, 1024], P(('tr', 'tc')), may hold values from -0.109375 to 0.109375
Outputs:
- layer_out: bfloat16 [65536, 1024], P('seq', ('tr', 'tc'))
Inputs may be any that keep to these rules, and one draw needn't show every extreme that they name: `seg_start`: 1 where a segment begins a prompt, 0 where it continues the prompt of the segment before; segment 0 begins a prompt; a prompt spans at most 32 segments, and in every draw one prompt spans exactly that many. `seg_len`: live tokens at the head of each segment; every segment of a prompt but its last is full. `memory_rates`: all three tables lie strictly between 0 and 1.
All inputs are finite; a program needn't handle non-finite values.
Results may differ from a plain program's by a relative error of at most 0.015.
Values may be sent and summed in bfloat16 or wider, within the bound.
No kernel may reach another device: no remote copies, remote signals or barrier semaphores. Data moves between devices by JAX's collectives and lax.ppermute only.
A program may use at most 192 MiB of HBM per device.

v0:
```python
import jax
import jax.numpy as jnp
from jax import lax
from jax.sharding import PartitionSpec as P

HD = 128
SEG = 1024
CONV = 4
PROMPT_SPAN = 32
epsilon = 1e-06
score_scale = 8.0


def passed_along(block, axis, distance):
    devices = range(lax.axis_size(axis))
    route = [(i - distance, i) for i in devices if i - distance in devices]
    return lax.ppermute(block, axis, route)


def passed_exact(block, axis, distance):
    high = block.astype(jnp.bfloat16)
    low = (block - high.astype(jnp.float32)).astype(jnp.bfloat16)
    high, low = passed_along((high, low), axis, distance)
    return high.astype(jnp.float32) + low.astype(jnp.float32)


def window_scan(seg_map, seg_shift, axis, reach):
    distance = 1
    while distance < reach:
        if 2 * distance >= reach:
            shift_before = passed_exact(seg_shift, axis, distance)
            seg_shift = exact_product(seg_map, shift_before) + seg_shift
        else:
            high = seg_shift.astype(jnp.bfloat16)
            low = (seg_shift - high.astype(jnp.float32)).astype(jnp.bfloat16)
            map_before, high, low = passed_along(
                (seg_map.astype(jnp.bfloat16), high, low), axis, distance
            )
            shift_before = high.astype(jnp.float32) + low.astype(jnp.float32)
            seg_shift = exact_product(seg_map, shift_before) + seg_shift
            seg_map = exact_product(seg_map, map_before.astype(jnp.float32))
        distance *= 2
    return seg_shift


def unit_rows(values_in):
    return values_in * lax.rsqrt(jnp.sum(values_in * values_in, -1, keepdims=True) + epsilon)


def exact_product(left, right):
    return jnp.matmul(left, right, precision=lax.Precision.HIGHEST)


def body(
    activations,
    seg_len,
    seg_start,
    memory_rates,
    w_qkv,
    conv_w,
    persistent,
    w_out,
    w_gate,
    w_up,
    w_down,
):
    token_rows, local_feat = activations.shape
    seg_count = seg_len.shape[0]
    full_width = w_qkv.shape[0]
    head_width = w_qkv.shape[2]
    local_heads = head_width // HD
    group_index = lax.axis_index(("tr", "tc"))
    wide = w_qkv.reshape(full_width, 3 * head_width)
    row_ids = jnp.arange(token_rows, dtype=jnp.int32)
    position = row_ids % SEG
    segment_of = row_ids // SEG
    continuing = seg_start[segment_of] == 0
    piece = lax.all_gather(activations, ("tr", "tc"), axis=1, tiled=True)
    piece_f = piece.astype(jnp.float32)
    projected = jnp.dot(piece, wide, preferred_element_type=jnp.float32)
    squares = jnp.sum(piece_f * piece_f, -1)
    qkv = (projected * lax.rsqrt(squares / full_width + epsilon)[:, None]).astype(jnp.bfloat16)
    edge_rows = passed_along(qkv[token_rows - (CONV - 1) :], "seq", 1)
    extended = jnp.concatenate([edge_rows, qkv], 0)
    taps = conv_w.reshape(CONV, 3 * head_width)
    convolved = jnp.zeros((token_rows, 3 * head_width), jnp.float32)
    for offset in range(CONV):
        shifted = extended[CONV - 1 - offset : CONV - 1 - offset + token_rows].astype(jnp.float32)
        valid = (position >= offset) | continuing
        convolved = convolved + jnp.where(valid[:, None], taps[offset] * shifted, 0.0)
    parts = convolved.reshape(token_rows, 3, local_heads, HD)
    query_n = unit_rows(parts[:, 0]).astype(jnp.bfloat16)
    key_n = unit_rows(parts[:, 1]).astype(jnp.bfloat16)
    value_n = parts[:, 2].astype(jnp.bfloat16)
    pkeys = unit_rows(persistent[0].astype(jnp.float32).reshape(-1, local_heads, HD)).astype(
        jnp.bfloat16
    )
    pvalues = persistent[1].reshape(-1, local_heads, HD)
    persist_rows = pkeys.shape[0]
    live = position < seg_len[segment_of]
    keys_live = jnp.where(live[:, None, None], key_n, jnp.zeros((), jnp.bfloat16)).reshape(
        seg_count, SEG, local_heads, HD
    )
    value_segs = value_n.reshape(seg_count, SEG, local_heads, HD)
    a_mats = jnp.einsum("cthi,cthj->chij", keys_live, keys_live, preferred_element_type=jnp.float32)
    b_mats = jnp.einsum(
        "cthi,cthj->chij", keys_live, value_segs, preferred_element_type=jnp.float32
    )
    my_rates = lax.dynamic_slice_in_dim(memory_rates, group_index * local_heads, local_heads, 2)
    decay_factor = my_rates[0][:, :, None, None]
    eta = my_rates[1][:, :, None, None]
    theta = my_rates[2][:, :, None, None]
    keep = (1 - seg_start).astype(jnp.float32)[:, None, None, None]
    identity = jnp.eye(HD, dtype=jnp.float32)
    upper = jnp.concatenate([(1.0 - decay_factor) * identity - theta * a_mats, eta * identity], -1)
    lower = jnp.concatenate([-theta * a_mats, eta * identity], -1)
    seg_maps = jnp.concatenate([upper, lower], -2) * keep
    seg_shifts = jnp.concatenate([theta * b_mats, theta * b_mats], -2)
    reach = min(PROMPT_SPAN, lax.axis_size("seq"))
    state_out = window_scan(seg_maps[0], seg_shifts[0], "seq", reach)
    memory_in = passed_exact(state_out[:, :HD], "seq", 1) * keep[0]
    query_seg = query_n.astype(jnp.float32)
    retr_parts = jnp.einsum("thi,hij->thj", query_seg, memory_in, precision=lax.Precision.HIGHEST)
    mem = retr_parts * lax.rsqrt(jnp.mean(retr_parts * retr_parts, -1, keepdims=True) + epsilon)
    block_rows = min(512, SEG)
    attn_parts = []
    seg_index = 0
    first = seg_index * SEG
    keys_all = jnp.concatenate([pkeys, key_n], 0)
    values_all = jnp.concatenate([pvalues, value_n], 0)
    cols_k = jnp.arange(persist_rows + SEG, dtype=jnp.int32)[None, :] - persist_rows
    for block_start in range(0, SEG, block_rows):
        query_blk = query_n[first + block_start : first + block_start + block_rows]
        scores = score_scale * jnp.einsum(
            "qhd,khd->hqk", query_blk, keys_all, preferred_element_type=jnp.float32
        )
        rows_q = block_start + jnp.arange(block_rows, dtype=jnp.int32)[:, None]
        allow = (cols_k < 0) | (cols_k <= rows_q) & (cols_k < seg_len[seg_index])
        weights = jnp.where(allow[None], jnp.exp(scores), 0.0)
        probs = (weights / jnp.sum(weights, -1, keepdims=True)).astype(jnp.bfloat16)
        attn_parts.append(
            jnp.einsum("hqk,khd->qhd", probs, values_all, preferred_element_type=jnp.float32)
        )
    attn = jnp.concatenate(attn_parts, 0)
    heads_out = (attn + mem).astype(jnp.bfloat16).reshape(token_rows, head_width)
    partial_value = jnp.dot(heads_out, w_out, preferred_element_type=jnp.float32)
    share = lax.psum_scatter(
        partial_value.astype(jnp.bfloat16), ("tr", "tc"), scatter_dimension=1, tiled=True
    ).astype(jnp.float32)
    resid = (activations.astype(jnp.float32) + share).astype(jnp.bfloat16)
    piece = lax.all_gather(resid, ("tr", "tc"), axis=1, tiled=True)
    piece_f = piece.astype(jnp.float32)
    gate = jnp.dot(piece, w_gate, preferred_element_type=jnp.float32)
    up_proj = jnp.dot(piece, w_up, preferred_element_type=jnp.float32)
    squares2 = jnp.sum(piece_f * piece_f, -1)
    inv_rms2 = lax.rsqrt(squares2 / full_width + epsilon)[:, None]
    hidden = (jax.nn.silu(gate * inv_rms2) * (up_proj * inv_rms2)).astype(jnp.bfloat16)
    down = jnp.dot(hidden, w_down, preferred_element_type=jnp.float32)
    ffn_share = lax.psum_scatter(
        down.astype(jnp.bfloat16), ("tr", "tc"), scatter_dimension=1, tiled=True
    ).astype(jnp.float32)
    return (resid.astype(jnp.float32) + ffn_share).astype(jnp.bfloat16)


def solution(mesh):
    return jax.shard_map(
        body,
        mesh=mesh,
        in_specs=(
            P("seq", ("tr", "tc")),
            P("seq"),
            P("seq"),
            P(None, "seq", None),
            P(None, None, ("tr", "tc")),
            P(None, None, ("tr", "tc")),
            P(None, None, ("tr", "tc")),
            P(("tr", "tc"), None),
            P(None, ("tr", "tc")),
            P(None, ("tr", "tc")),
            P(("tr", "tc"), None),
        ),
        out_specs=P("seq", ("tr", "tc")),
        check_vma=False,
    )
```

profile of v0, /device:TPU:1, one launch (start us, length us, event | category | flops | bytes accessed | tf_op | source)
XLA Modules:
  0.0 371.0 jit_solution(2655117677076065765)
XLA Ops:
  6.5 0.7 all-gather.3.cloned.1.call-update
  8.6 0.7 fusion.86
  9.5 2.6 copy.76
  12.1 0.6 fusion.69
  12.7 0.7 fusion.83
  13.6 0.7 broadcast_multiply_fusion
  14.3 2.0 fusion.7
  16.3 46.8 %all-gather.3.cloned.1.call-done = bf16[1024,1024]{1,0:T(8,128)(2,1)} async-done(((bf16[1024,256]{1,0:T(8,128)(2,1)}), bf16[1024,1024]{1,0:T(8,128)(2,1)}) %all-gather.3.cloned.1.call-update) | async-done | bytes 2097168 | tf_op jit(solution)/shard_map/all_gather | solution.py:78
  63.1 2.1 multiply_reduce_fusion.1
  65.2 3.9 %multiply_convert_fusion = bf16[1024,768]{1,0:T(8,128)(2,1)S(1)} fusion(bf16[1024,1024]{1,0:T(8,128)(2,1)} %all-gather.3.cloned.1.call-done, bf16[1024,768]{0,1:T(8,128)(2,1)} %bitcast.82, f32[1024]{0:T(1024)S(1)} %add_rsqrt_fusion.4), kind=kOutput, calls=%fused_computation.11 | convolution fusion | flops 1612185600 | bytes 5246976 | tf_op jit(solution)/shard_map/dot_general | solution.py:80
  69.1 3.6 collective-permute-start
  72.7 0.6 fusion.57
  73.5 3.8 %select_add_fusion = f32[1024,768]{1,0:T(8,128)} fusion(bf16[1024,768]{1,0:T(8,128)(2,1)S(1)} %multiply_convert_fusion, bf16[3,768]{1,0:T(4,128)(2,1)S(1)} %collective-permute-done, f32[768]{0:T(1024)S(1)} %mul.251, f32[768]{0:T(1024)S(1)} %mul.248, f32[768]{0:T(1024)S(1)} %mul.245, f32[768]{0:T(1024)S(1)} %mul.239, ...), kind=kLoop, calls=%fused_computation.10 | loop fusion | flops 18874368 | bytes 4739584 | tf_op jit(solution)/shard_map/add | solution.py:90
  77.3 5.2 %reshape.298 = f32[1024,3,2,128]{3,2,1,0:T(2,128)} reshape(f32[1024,768]{1,0:T(8,128)} %select_add_fusion) | data formatting | bytes 6291456 | tf_op jit(solution)/shard_map/reshape | solution.py:91
  82.5 1.6 slice.86
  84.1 1.7 fusion.85
  85.9 0.4 multiply_reduce_fusion.3
  86.7 0.5 fusion.14
  87.2 0.7 fusion.24
  88.6 4.2 %collective-permute-start.5 = (bf16[2,256,128]{1,2,0:T(8,128)(2,1)}, bf16[2,256,128]{1,2,0:T(8,128)(2,1)}, u32[]{:S(2)}, u32[]{:S(2)}) collective-permute-start(bf16[2,256,128]{1,2,0:T(8,128)(2,1)} %fusion.24), channel_id=1, source_target_pairs={{0,4},{4,8},{8,12},{12,16},{16,20},{20,24},{24,28},{28,32},{32,36}... | collective-permute-start | bytes 393224 | tf_op jit(solution)/shard_map/ppermute | solution.py:17
  92.8 1.9 collective-permute-start.6
  94.8 0.6 subtract_bitcast_fusion
  95.5 0.7 fusion.18
  96.2 3.5 collective-permute-start.1
  99.8 3.0 fusion.3
  102.8 2.9 fusion.1
  105.7 4.5 %fusion.12 = f32[512,2,128]{0,2,1:T(8,128)S(1)} fusion(f32[2,512,1040]{1,2,0:T(8,128)} %fusion.3, bf16[1024,2,128]{2,0,1:T(8,128)(2,1)} %bitcast.84, bf16[16,2,128]{2,0,1:T(8,128)(2,1)S(1)} %copy.78), kind=kOutput, calls=%fused_computation.29 | convolution fusion | flops 275826688 | bytes 5316608 | tf_op jit(solution)/shard_map/hqk,khd->qhd/dot_general | solution.py:142
  110.3 1.5 subtract_convert_fusion.3
  111.8 3.2 collective-permute-start.8
  115.0 5.8 %collective-permute-start.7 = (bf16[2,256,128]{1,2,0:T(8,128)(2,1)S(1)}, bf16[2,256,128]{1,2,0:T(8,128)(2,1)S(1)}, u32[]{:S(2)}, u32[]{:S(2)}) collective-permute-start(bf16[2,256,128]{1,2,0:T(8,128)(2,1)S(1)} %get-tuple-element.18), channel_id=1, source_target_pairs={{0,8},{4,12},{8,16},{12,20},{16,24},{20,28},{24,32},{28,36},{32,40... | collective-permute-start | bytes 393224 | tf_op jit(solution)/shard_map/ppermute | solution.py:17
  120.8 0.6 fusion.87
  121.4 1.9 collective-permute-start.2
  123.4 0.7 subtract_convert_fusion.2
  124.1 3.5 collective-permute-start.10
  127.6 3.6 collective-permute-start.9
  131.2 0.4 fusion.88
  131.6 2.3 collective-permute-start.3
  133.8 5.3 %collective-permute-done.9 = bf16[2,256,128]{1,2,0:T(8,128)(2,1)S(1)} collective-permute-done((bf16[2,256,128]{1,2,0:T(8,128)(2,1)S(1)}, bf16[2,256,128]{1,2,0:T(8,128)(2,1)S(1)}, u32[]{:S(2)}, u32[]{:S(2)}) %collective-permute-start.9) | collective-permute-done | bytes 131104 | tf_op jit(solution)/shard_map/ppermute | solution.py:17
  139.1 0.7 subtract_convert_fusion.1
  139.8 8.8 %collective-permute-start.12 = (bf16[2,256,128]{1,2,0:T(8,128)(2,1)S(1)}, bf16[2,256,128]{1,2,0:T(8,128)(2,1)S(1)}, u32[]{:S(2)}, u32[]{:S(2)}) collective-permute-start(bf16[2,256,128]{1,2,0:T(8,128)(2,1)S(1)} %get-tuple-element.13), channel_id=1, source_target_pairs={{0,32},{4,36},{8,40},{12,44},{16,48},{20,52},{24,56},{28,60},{32,6... | collective-permute-start | bytes 393224 | tf_op jit(solution)/shard_map/ppermute | solution.py:17
  148.7 8.0 %collective-permute-start.11 = (bf16[2,256,128]{1,2,0:T(8,128)(2,1)S(1)}, bf16[2,256,128]{1,2,0:T(8,128)(2,1)S(1)}, u32[]{:S(2)}, u32[]{:S(2)}) collective-permute-start(bf16[2,256,128]{1,2,0:T(8,128)(2,1)S(1)} %get-tuple-element.14), channel_id=1, source_target_pairs={{0,32},{4,36},{8,40},{12,44},{16,48},{20,52},{24,56},{28,60},{32,6... | collective-permute-start | bytes 393224 | tf_op jit(solution)/shard_map/ppermute | solution.py:17
  156.7 0.4 fusion.89
  157.1 2.1 collective-permute-start.4
  159.2 1.4 collective-permute-done.11
  160.6 0.7 subtract_convert_fusion
  161.3 6.2 %collective-permute-start.14 = (bf16[2,256,128]{1,2,0:T(8,128)(2,1)S(1)}, bf16[2,256,128]{1,2,0:T(8,128)(2,1)S(1)}, u32[]{:S(2)}, u32[]{:S(2)}) collective-permute-start(bf16[2,256,128]{1,2,0:T(8,128)(2,1)S(1)} %get-tuple-element.11), channel_id=1, source_target_pairs={{0,64},{4,68},{8,72},{12,76},{16,80},{20,84},{24,88},{28,92},{32,9... | collective-permute-start | bytes 393224 | tf_op jit(solution)/shard_map/ppermute | solution.py:17
  167.5 3.4 collective-permute-start.13
  170.9 0.4 fusion.90
  171.3 2.4 collective-permute-done.13
  173.7 0.7 fusion.26
  174.4 4.2 %collective-permute-start.16 = (bf16[2,128,128]{1,2,0:T(8,128)(2,1)S(1)}, bf16[2,128,128]{1,2,0:T(8,128)(2,1)S(1)}, u32[]{:S(2)}, u32[]{:S(2)}) collective-permute-start(bf16[2,128,128]{1,2,0:T(8,128)(2,1)S(1)} %get-tuple-element.9), channel_id=1, source_target_pairs={{0,4},{4,8},{8,12},{12,16},{16,20},{20,24},{24,28},{28,32},{32,36}... | collective-permute-start | bytes 196616 | tf_op jit(solution)/shard_map/ppermute | solution.py:17
  178.7 1.9 collective-permute-start.15
  180.6 4.5 %fusion.13 = f32[512,2,128]{0,2,1:T(8,128)S(1)} fusion(f32[2,512,1040]{1,2,0:T(8,128)} %fusion.1, bf16[1024,2,128]{2,0,1:T(8,128)(2,1)} %bitcast.85, bf16[16,2,128]{2,0,1:T(8,128)(2,1)S(1)} %copy.78), kind=kOutput, calls=%fused_computation.30 | convolution fusion | flops 275826688 | bytes 5316608 | tf_op jit(solution)/shard_map/hqk,khd->qhd/dot_general | solution.py:142
  185.5 1.3 collective-permute-done.15
  186.8 0.6 multiply_reduce_fusion.2
  187.7 2.1 convolution_convert_fusion
  189.8 54.3 %reduce-scatter.3.cloned.1.call-done = bf16[1024,256]{1,0:T(8,128)(2,1)} async-done(((bf16[1024,1024]{1,0:T(8,128)(2,1)}), bf16[1024,256]{1,0:T(8,128)(2,1)}) %reduce-scatter.3.cloned.1.call-update) | async-done | bytes 524304 | tf_op jit(solution)/shard_map/reduce_scatter | solution.py:147
  244.1 2.0 add_convert_fusion.1
  246.4 50.0 %all-gather.5.cloned.1.call-done = bf16[1024,1024]{1,0:T(8,128)(2,1)} async-done(((bf16[1024,256]{1,0:T(8,128)(2,1)}), bf16[1024,1024]{1,0:T(8,128)(2,1)}) %all-gather.5.cloned.1.call-update) | async-done | bytes 2097168 | tf_op jit(solution)/shard_map/all_gather | solution.py:151
  296.4 2.1 multiply_reduce_fusion
  298.5 4.9 %fusion.91 = f32[1024,704]{0,1:T(8,128)} fusion(bf16[1024,1024]{1,0:T(8,128)(2,1)} %all-gather.5.cloned.1.call-done, bf16[1024,704]{0,1:T(8,128)(2,1)S(1)} %copy-done.15), kind=kOutput, calls=%fused_computation.159 | convolution fusion | flops 1476395008 | bytes 6422528 | tf_op jit(solution)/shard_map/dot_general | solution.py:153
  303.4 7.8 %convolution_convert_fusion.1 = bf16[1024,1024]{1,0:T(8,128)(2,1)} fusion(bf16[704,1024]{1,0:T(8,128)(2,1)S(1)} %copy-done, f32[1024,704]{0,1:T(8,128)} %fusion.91, bf16[1024,1024]{1,0:T(8,128)(2,1)} %all-gather.5.cloned.1.call-done, bf16[1024,704]{0,1:T(8,128)(2,1)} %param.20, f32[1024]{0:T(1024)S(1)} %add_rsqrt_fusion.3), kind=kOutput, calls=%fused_computation.22 | convolution fusion | flops 2959605760 | bytes 9965568 | tf_op jit(solution)/shard_map/dot_general | solution.py:158
  311.3 51.2 %reduce-scatter.5.cloned.1.call-done = bf16[1024,256]{1,0:T(8,128)(2,1)} async-done(((bf16[1024,1024]{1,0:T(8,128)(2,1)}), bf16[1024,256]{1,0:T(8,128)(2,1)}) %reduce-scatter.5.cloned.1.call-update) | async-done | bytes 524304 | tf_op jit(solution)/shard_map/reduce_scatter | solution.py:159
  362.5 2.0 add_convert_fusion
  (86 shorter events, 2.8 us)
Async XLA Ops:
  6.5 296.9 %copy-start = (bf16[704,1024]{1,0:T(8,128)(2,1)S(1)}, bf16[704,1024]{1,0:T(8,128)(2,1)}, u32[]{:S(2)}) copy-start(bf16[704,1024]{1,0:T(8,128)(2,1)} %param.21) | copy-start | bytes 4325380
  6.5 5.6 %copy-start.11 = (f32[3,1,8]{2,1,0:T(1,128)S(1)}, f32[3,1,8]{2,1,0:T(1,128)}, u32[]{:S(2)}) copy-start(f32[3,1,8]{2,1,0:T(1,128)} %param.14) | copy-start | bytes 292
  6.5 6.9 %copy-start.10 = (f32[4,3,256]{2,0,1:T(4,128)S(1)}, f32[4,3,256]{2,0,1:T(4,128)}, u32[]{:S(2)}) copy-start(f32[4,3,256]{2,0,1:T(4,128)} %param.16) | copy-start | bytes 36868
  6.5 56.6 %all-gather.3.cloned.1.call-start = ((), (), s32[]{:S(2)}) async-start(), calls=%async_computation.2 | async-start | bytes 2621440 | tf_op jit(solution)/shard_map/all_gather | solution.py:78
  7.3 236.9 %reduce-scatter.3.cloned.1.call-start = ((), (), s32[]{:S(2)}) async-start(), calls=%async_computation.3 | async-start | bytes 2621440 | tf_op jit(solution)/shard_map/reduce_scatter | solution.py:147
  13.5 55.6 %copy-start.8 = (f32[128,128]{0,1:T(8,128)}, f32[128,128]{0,1:T(8,128)S(1)}, u32[]{:S(2)}) copy-start(f32[128,128]{0,1:T(8,128)S(1)} %fusion.50) | copy-start | bytes 196612
  69.1 4.4 %collective-permute-start = (bf16[3,768]{1,0:T(4,128)(2,1)S(1)}, bf16[3,768]{1,0:T(4,128)(2,1)S(1)}, u32[]{:S(2)}, u32[]{:S(2)}) collective-permute-start(bf16[3,768]{1,0:T(4,128)(2,1)S(1)} %slice.81), channel_id=1, source_target_pairs={{0,4},{4,8},{8,12},{12,16},{16,20},{20,24},{24,28},{28,32},{32,36}... | collective-permute-start | bytes 13832 | tf_op jit(solution)/shard_map/ppermute | solution.py:17
  85.8 0.9 copy-start.13
  85.8 0.9 copy-start.16
  85.9 2.7 copy-start.6
  86.3 8.5 %copy-start.9 = (f32[128,128]{0,1:T(8,128)S(1)}, f32[128,128]{0,1:T(8,128)}, u32[]{:S(2)}) copy-start(f32[128,128]{0,1:T(8,128)} %copy-done.8) | copy-start | bytes 196612
  86.3 8.5 %copy-start.12 = (f32[2]{0:T(128)S(1)}, f32[2]{0:T(128)}, u32[]{:S(2)}) copy-start(f32[2]{0:T(128)} %get-tuple-element.19) | copy-start | bytes 28
  86.3 8.5 %copy-start.14 = (f32[2]{0:T(128)S(1)}, f32[2]{0:T(128)}, u32[]{:S(2)}) copy-start(f32[2]{0:T(128)} %get-tuple-element.31) | copy-start | bytes 28
  86.7 8.7 %copy-start.5 = (f32[1,2,128,128]{2,3,1,0:T(8,128)S(1)}, f32[1,2,128,128]{2,3,1,0:T(8,128)}, u32[]{:S(2)}) copy-start(f32[1,2,128,128]{2,3,1,0:T(8,128)} %broadcast_multiply_fusion) | copy-start | bytes 393220
  87.9 11.9 %copy-start.4 = (pred[512,1040]{0,1:T(8,128)(4,1)S(1)}, pred[512,1040]{0,1:T(8,128)(4,1)}, u32[]{:S(2)}) copy-start(pred[512,1040]{0,1:T(8,128)(4,1)} %get-tuple-element.30) | copy-start | bytes 1597444
  88.6 21.7 %collective-permute-start.5 = (bf16[2,256,128]{1,2,0:T(8,128)(2,1)}, bf16[2,256,128]{1,2,0:T(8,128)(2,1)}, u32[]{:S(2)}, u32[]{:S(2)}) collective-permute-start(bf16[2,256,128]{1,2,0:T(8,128)(2,1)} %fusion.24), channel_id=1, source_target_pairs={{0,4},{4,8},{8,12},{12,16},{16,20},{20,24},{24,28},{28,32},{32,36}... | collective-permute-start | bytes 393224 | tf_op jit(solution)/shard_map/ppermute | solution.py:17
  92.8 17.5 %collective-permute-start.6 = (bf16[2,256,128]{1,2,0:T(8,128)(2,1)S(1)}, bf16[2,256,128]{1,2,0:T(8,128)(2,1)}, u32[]{:S(2)}, u32[]{:S(2)}) collective-permute-start(bf16[2,256,128]{1,2,0:T(8,128)(2,1)S(1)} %fusion.25), channel_id=1, source_target_pairs={{0,4},{4,8},{8,12},{12,16},{16,20},{20,24},{24,28},{28,32},{32,36}... | collective-permute-start | bytes 393224 | tf_op jit(solution)/shard_map/ppermute | solution.py:17
  96.2 24.6 %collective-permute-start.1 = (bf16[2,256,256]{1,2,0:T(8,128)(2,1)}, bf16[2,256,256]{1,2,0:T(8,128)(2,1)S(1)}, u32[]{:S(2)}, u32[]{:S(2)}) collective-permute-start(bf16[2,256,256]{1,2,0:T(8,128)(2,1)} %fusion.18), channel_id=1, source_target_pairs={{0,4},{4,8},{8,12},{12,16},{16,20},{20,24},{24,28},{28,32},{32,36}... | collective-permute-start | bytes 786440 | tf_op jit(solution)/shard_map/ppermute | solution.py:17
  99.8 3.0 copy-start.3
  111.8 11.6 %collective-permute-start.8 = (bf16[2,256,128]{1,2,0:T(8,128)(2,1)S(1)}, bf16[2,256,128]{1,2,0:T(8,128)(2,1)S(1)}, u32[]{:S(2)}, u32[]{:S(2)}) collective-permute-start(bf16[2,256,128]{1,2,0:T(8,128)(2,1)S(1)} %get-tuple-element.17), channel_id=1, source_target_pairs={{0,8},{4,12},{8,16},{12,20},{16,24},{20,28},{24,32},{28,36},{32,40... | collective-permute-start | bytes 393224 | tf_op jit(solution)/shard_map/ppermute | solution.py:17
  115.0 8.4 %collective-permute-start.7 = (bf16[2,256,128]{1,2,0:T(8,128)(2,1)S(1)}, bf16[2,256,128]{1,2,0:T(8,128)(2,1)S(1)}, u32[]{:S(2)}, u32[]{:S(2)}) collective-permute-start(bf16[2,256,128]{1,2,0:T(8,128)(2,1)S(1)} %get-tuple-element.18), channel_id=1, source_target_pairs={{0,8},{4,12},{8,16},{12,20},{16,24},{20,28},{24,32},{28,36},{32,40... | collective-permute-start | bytes 393224 | tf_op jit(solution)/shard_map/ppermute | solution.py:17
  121.4 9.7 %collective-permute-start.2 = (bf16[2,256,256]{2,1,0:T(8,128)(2,1)S(1)}, bf16[2,256,256]{2,1,0:T(8,128)(2,1)S(1)}, u32[]{:S(2)}, u32[]{:S(2)}) collective-permute-start(bf16[2,256,256]{2,1,0:T(8,128)(2,1)S(1)} %get-tuple-element.34), channel_id=1, source_target_pairs={{0,8},{4,12},{8,16},{12,20},{16,24},{20,28},{24,32},{28,36},{32,40... | collective-permute-start | bytes 786440 | tf_op jit(solution)/shard_map/ppermute | solution.py:17
  124.1 9.8 %collective-permute-start.10 = (bf16[2,256,128]{1,2,0:T(8,128)(2,1)S(1)}, bf16[2,256,128]{1,2,0:T(8,128)(2,1)S(1)}, u32[]{:S(2)}, u32[]{:S(2)}) collective-permute-start(bf16[2,256,128]{1,2,0:T(8,128)(2,1)S(1)} %get-tuple-element.15), channel_id=1, source_target_pairs={{0,16},{4,20},{8,24},{12,28},{16,32},{20,36},{24,40},{28,44},{32,4... | collective-permute-start | bytes 393224 | tf_op jit(solution)/shard_map/ppermute | solution.py:17
  127.6 11.6 %collective-permute-start.9 = (bf16[2,256,128]{1,2,0:T(8,128)(2,1)S(1)}, bf16[2,256,128]{1,2,0:T(8,128)(2,1)S(1)}, u32[]{:S(2)}, u32[]{:S(2)}) collective-permute-start(bf16[2,256,128]{1,2,0:T(8,128)(2,1)S(1)} %get-tuple-element.16), channel_id=1, source_target_pairs={{0,16},{4,20},{8,24},{12,28},{16,32},{20,36},{24,40},{28,44},{32,4... | collective-permute-start | bytes 393224 | tf_op jit(solution)/shard_map/ppermute | solution.py:17
  131.6 25.2 %collective-permute-start.3 = (bf16[2,256,256]{2,1,0:T(8,128)(2,1)S(1)}, bf16[2,256,256]{2,1,0:T(8,128)(2,1)S(1)}, u32[]{:S(2)}, u32[]{:S(2)}) collective-permute-start(bf16[2,256,256]{2,1,0:T(8,128)(2,1)S(1)} %get-tuple-element.37), channel_id=1, source_target_pairs={{0,16},{4,20},{8,24},{12,28},{16,32},{20,36},{24,40},{28,44},{32,4... | collective-permute-start | bytes 786440 | tf_op jit(solution)/shard_map/ppermute | solution.py:17
  139.8 19.4 %collective-permute-start.12 = (bf16[2,256,128]{1,2,0:T(8,128)(2,1)S(1)}, bf16[2,256,128]{1,2,0:T(8,128)(2,1)S(1)}, u32[]{:S(2)}, u32[]{:S(2)}) collective-permute-start(bf16[2,256,128]{1,2,0:T(8,128)(2,1)S(1)} %get-tuple-element.13), channel_id=1, source_target_pairs={{0,32},{4,36},{8,40},{12,44},{16,48},{20,52},{24,56},{28,60},{32,6... | collective-permute-start | bytes 393224 | tf_op jit(solution)/shard_map/ppermute | solution.py:17
  148.7 11.9 %collective-permute-start.11 = (bf16[2,256,128]{1,2,0:T(8,128)(2,1)S(1)}, bf16[2,256,128]{1,2,0:T(8,128)(2,1)S(1)}, u32[]{:S(2)}, u32[]{:S(2)}) collective-permute-start(bf16[2,256,128]{1,2,0:T(8,128)(2,1)S(1)} %get-tuple-element.14), channel_id=1, source_target_pairs={{0,32},{4,36},{8,40},{12,44},{16,48},{20,52},{24,56},{28,60},{32,6... | collective-permute-start | bytes 393224 | tf_op jit(solution)/shard_map/ppermute | solution.py:17
  157.1 13.7 %collective-permute-start.4 = (bf16[2,256,256]{2,1,0:T(8,128)(2,1)S(1)}, bf16[2,256,256]{2,1,0:T(8,128)(2,1)S(1)}, u32[]{:S(2)}, u32[]{:S(2)}) collective-permute-start(bf16[2,256,256]{2,1,0:T(8,128)(2,1)S(1)} %get-tuple-element.40), channel_id=1, source_target_pairs={{0,32},{4,36},{8,40},{12,44},{16,48},{20,52},{24,56},{28,60},{32,6... | collective-permute-start | bytes 786440 | tf_op jit(solution)/shard_map/ppermute | solution.py:17
  161.3 10.0 %collective-permute-start.14 = (bf16[2,256,128]{1,2,0:T(8,128)(2,1)S(1)}, bf16[2,256,128]{1,2,0:T(8,128)(2,1)S(1)}, u32[]{:S(2)}, u32[]{:S(2)}) collective-permute-start(bf16[2,256,128]{1,2,0:T(8,128)(2,1)S(1)} %get-tuple-element.11), channel_id=1, source_target_pairs={{0,64},{4,68},{8,72},{12,76},{16,80},{20,84},{24,88},{28,92},{32,9... | collective-permute-start | bytes 393224 | tf_op jit(solution)/shard_map/ppermute | solution.py:17
  167.5 6.2 %collective-permute-start.13 = (bf16[2,256,128]{1,2,0:T(8,128)(2,1)S(1)}, bf16[2,256,128]{1,2,0:T(8,128)(2,1)S(1)}, u32[]{:S(2)}, u32[]{:S(2)}) collective-permute-start(bf16[2,256,128]{1,2,0:T(8,128)(2,1)S(1)} %get-tuple-element.12), channel_id=1, source_target_pairs={{0,64},{4,68},{8,72},{12,76},{16,80},{20,84},{24,88},{28,92},{32,9... | collective-permute-start | bytes 393224 | tf_op jit(solution)/shard_map/ppermute | solution.py:17
  174.4 11.1 %collective-permute-start.16 = (bf16[2,128,128]{1,2,0:T(8,128)(2,1)S(1)}, bf16[2,128,128]{1,2,0:T(8,128)(2,1)S(1)}, u32[]{:S(2)}, u32[]{:S(2)}) collective-permute-start(bf16[2,128,128]{1,2,0:T(8,128)(2,1)S(1)} %get-tuple-element.9), channel_id=1, source_target_pairs={{0,4},{4,8},{8,12},{12,16},{16,20},{20,24},{24,28},{28,32},{32,36}... | collective-permute-start | bytes 196616 | tf_op jit(solution)/shard_map/ppermute | solution.py:17
  178.7 8.1 %collective-permute-start.15 = (bf16[2,128,128]{1,2,0:T(8,128)(2,1)S(1)}, bf16[2,128,128]{1,2,0:T(8,128)(2,1)S(1)}, u32[]{:S(2)}, u32[]{:S(2)}) collective-permute-start(bf16[2,128,128]{1,2,0:T(8,128)(2,1)S(1)} %get-tuple-element.10), channel_id=1, source_target_pairs={{0,4},{4,8},{8,12},{12,16},{16,20},{20,24},{24,28},{28,32},{32,36}... | collective-permute-start | bytes 196616 | tf_op jit(solution)/shard_map/ppermute | solution.py:17
  185.1 2.5 copy-start.7
  187.7 56.5 %copy-start.2 = (bf16[1024,256]{1,0:T(8,128)(2,1)S(1)}, bf16[1024,256]{1,0:T(8,128)(2,1)}, u32[]{:S(2)}) copy-start(bf16[1024,256]{1,0:T(8,128)(2,1)} %param.11) | copy-start | bytes 1572868
  189.8 108.8 %copy-start.15 = (bf16[1024,704]{0,1:T(8,128)(2,1)S(1)}, bf16[1024,704]{0,1:T(8,128)(2,1)}, u32[]{:S(2)}) copy-start(bf16[1024,704]{0,1:T(8,128)(2,1)} %param.19) | copy-start | bytes 4325380
  189.8 106.6 %all-gather.5.cloned.1.call-start = ((), (), s32[]{:S(2)}) async-start(), calls=%async_computation.4 | async-start | bytes 2621440 | tf_op jit(solution)/shard_map/all_gather | solution.py:151
  246.1 116.4 %reduce-scatter.5.cloned.1.call-start = ((), (), s32[]{:S(2)}) async-start(), calls=%async_computation.5 | async-start | bytes 2621440 | tf_op jit(solution)/shard_map/reduce_scatter | solution.py:159
  303.4 59.1 %copy-start.1 = (bf16[1024,256]{1,0:T(8,128)(2,1)S(1)}, bf16[1024,256]{1,0:T(8,128)(2,1)}, u32[]{:S(2)}) copy-start(bf16[1024,256]{1,0:T(8,128)(2,1)} %add_convert_fusion.1) | copy-start | bytes 1572868
Sparse Core Ops, SparseCore 0:
  9.1 53.9 all-gather.2
  189.9 54.1 reduce-scatter.2
  246.2 50.1 all-gather.4
  311.4 51.0 reduce-scatter.4
where the time goes:
time: 372 us; the launch traced here: 371 us
  waiting for transfers between devices  214 us (58%)
  starting transfers between devices  68.5 us (18%)
  matrix products  41.4 us (11%)
  other arithmetic  20.5 us (6%)
  between operations  15.1 us (4%)
  local copies, waits for them, and re-layouts  11.4 us (3%)
    ppermute x17, starting transfers between devices, passed_along(): return lax.ppermute(block, axis, route)  68.2 us
    reduce_scatter x1, waiting for transfers between devices, body(): lax.psum_scatter(partial_value.astype(jnp.bfloat16), ('tr', 'tc'), scatte...  54.3 us
    reduce_scatter x1, waiting for transfers between devices, body(): lax.psum_scatter(down.astype(jnp.bfloat16), ('tr', 'tc'), scatter_dimensi...  51.2 us
    all_gather x1, waiting for transfers between devices, body(): piece = lax.all_gather(resid, ('tr', 'tc'), axis=1, tiled=True)  50 us
    all_gather x1, waiting for transfers between devices, body(): piece = lax.all_gather(activations, ('tr', 'tc'), axis=1, tiled=True)  46.8 us
    ppermute x17, waiting for transfers between devices, passed_along(): return lax.ppermute(block, axis, route)  10.9 us
    dot_general x2, matrix products, body(): jnp.einsum('hqk,khd->qhd', probs, values_all, preferred_element_type=jnp....  9.03 us
    dot_general x1, matrix products, body(): down = jnp.dot(hidden, w_down, preferred_element_type=jnp.float32)  7.8 us
  transfers between devices with their start and end apart: 21, of which 10 were waited for; matrix products, arithmetic and copies ran while one was open for 8% of the time, Pallas kernels for 0%

commit v1 on v0

--- a/solution.py
+++ b/solution.py
@@ -75,7 +75,10 @@
     position = row_ids % SEG
     segment_of = row_ids // SEG
     continuing = seg_start[segment_of] == 0
-    piece = lax.all_gather(activations, ("tr", "tc"), axis=1, tiled=True)
+    piece = jnp.concatenate(
+        lax.all_to_all(jnp.stack([activations] * lax.axis_size(("tr", "tc"))), ("tr", "tc"), 0, 0),
+        axis=1,
+    )
     piece_f = piece.astype(jnp.float32)
     projected = jnp.dot(piece, wide, preferred_element_type=jnp.float32)
     squares = jnp.sum(piece_f * piece_f, -1)

time: 372 us -> 357 us (0.960)
  waiting for transfers between devices: 214 us -> 167 us
  starting transfers between devices: 68.5 us -> 84.1 us
  local copies, waits for them, and re-layouts: 11.4 us -> 20.4 us
  other arithmetic: 20.5 us -> 28.5 us
    all_gather x1 -> x0, waiting for transfers between devices: 46.8 us -> none  [body(): piece = lax.all_gather(activations, ('tr', 'tc'), axis=1, tiled=True)]
    ppermute x17, starting transfers between devices: 68.2 us -> 79 us  [passed_along(): return lax.ppermute(block, axis, route)]
    all_to_all x0 -> x1, waiting for transfers between devices: none -> 7.03 us  [body(): lax.all_to_all(jnp.stack([activations] * lax.axis_size(('tr', 'tc'))), ('...]
    ppermute x17, waiting for transfers between devices: 10.9 us -> 3.95 us  [passed_along(): return lax.ppermute(block, axis, route)]
    all_to_all x0 -> x1, starting transfers between devices: none -> 4.83 us  [body(): lax.all_to_all(jnp.stack([activations] * lax.axis_size(('tr', 'tc'))), ('...]
  transfers between devices with their start and end apart: 21 -> 21, of which waited for: 10 -> 6; matrix products, arithmetic and copies ran while one was open for 8% -> 12% of each run, Pallas kernels for 0% -> 0%
where the time goes in v1:
time: 357 us; the launch traced here: 356 us
  waiting for transfers between devices  167 us (47%)
  starting transfers between devices  84.1 us (24%)
  matrix products  40.9 us (11%)
  other arithmetic  28.5 us (8%)
  local copies, waits for them, and re-layouts  20.4 us (6%)
  between operations  15.1 us (4%)
    ppermute x17, starting transfers between devices, passed_along(): return lax.ppermute(block, axis, route)  79 us
    reduce_scatter x1, waiting for transfers between devices, body(): lax.psum_scatter(partial_value.astype(jnp.bfloat16), ('tr', 'tc'), scatte...  54.7 us
    reduce_scatter x1, waiting for transfers between devices, body(): lax.psum_scatter(down.astype(jnp.bfloat16), ('tr', 'tc'), scatter_dimensi...  51.2 us
    all_gather x1, waiting for transfers between devices, body(): piece = lax.all_gather(resid, ('tr', 'tc'), axis=1, tiled=True)  50.1 us
    dot_general x2, matrix products, body(): jnp.einsum('hqk,khd->qhd', probs, values_all, preferred_element_type=jnp....  9.03 us
    dot_general x1, matrix products, body(): down = jnp.dot(hidden, w_down, preferred_element_type=jnp.float32)  7.79 us
    add x1, other arithmetic, body(): convolved + jnp.where(valid[:, None], taps[offset] * shifted, 0.0)  7.24 us
  transfers between devices with their start and end apart: 21, of which 6 were waited for; matrix products, arithmetic and copies ran while one was open for 12% of the time, Pallas kernels for 0%

profile of v1, /device:TPU:1, one launch (start us, length us, event | category | flops | bytes accessed | tf_op | source)
XLA Modules:
  0.0 356.1 jit_solution(9158407504251448679)
XLA Ops:
  6.5 1.4 copy.78
  7.9 1.6 stack.2
  9.5 4.8 %all-to-all-start = ((bf16[4,1024,256]{1,2,0:T(8,128)(2,1)}), bf16[4,1024,256]{1,2,0:T(8,128)(2,1)S(1)}, u32[]{:S(2)}, u32[]{:S(2)}) async-start(bf16[4,1024,256]{1,2,0:T(8,128)(2,1)} %stack.2), calls=%async_computation | async-start | bytes 4194304 | tf_op jit(solution)/shard_map/all_to_all | solution.py:79
  19.3 0.7 reshape.310
  20.0 0.7 multiply_reduce_fusion.5
  20.7 1.3 copy.83
  22.0 2.6 copy.79
  24.6 1.3 fusion.69
  25.9 1.3 fusion.83
  27.2 1.5 slice_reduce_fusion.3
  28.7 0.7 add_rsqrt_fusion.5
  29.4 0.7 fusion.52
  30.1 0.7 broadcast_multiply_fusion
  30.8 2.7 fusion.7
  33.5 7.0 %all-to-all-done = bf16[4,1024,256]{1,2,0:T(8,128)(2,1)S(1)} async-done(((bf16[4,1024,256]{1,2,0:T(8,128)(2,1)}), bf16[4,1024,256]{1,2,0:T(8,128)(2,1)S(1)}, u32[]{:S(2)}, u32[]{:S(2)}) %all-to-all-start) | async-done | bytes 2097184 | tf_op jit(solution)/shard_map/all_to_all | solution.py:79
  41.1 3.3 multiply_convert_fusion
  44.4 1.2 copy-done.3
  45.6 4.2 %collective-permute-start = (bf16[3,768]{1,0:T(4,128)(2,1)S(1)}, bf16[3,768]{1,0:T(4,128)(2,1)S(1)}, u32[]{:S(2)}, u32[]{:S(2)}) collective-permute-start(bf16[3,768]{1,0:T(4,128)(2,1)S(1)} %slice.81), channel_id=1, source_target_pairs={{0,4},{4,8},{8,12},{12,16},{16,20},{20,24},{24,28},{28,32},{32,36}... | collective-permute-start | bytes 13832 | tf_op jit(solution)/shard_map/ppermute | solution.py:17
  49.8 0.7 mul.240
  50.5 0.7 mul.246
  51.2 7.2 %select_add_fusion = f32[1024,768]{1,0:T(8,128)} fusion(bf16[1024,768]{1,0:T(8,128)(2,1)} %copy-done.3, bf16[3,768]{1,0:T(4,128)(2,1)S(1)} %collective-permute-done, f32[768]{0:T(1024)S(1)} %mul.252, f32[768]{0:T(1024)S(1)} %mul.249, f32[768]{0:T(1024)S(1)} %mul.246, f32[768]{0:T(1024)S(1)} %mul.240, pred[1024]{0:T(1024)(128)(4,1)} %get-tuple-element.48, ...), kind=kLoop, calls=%fused_computation.10 | loop fusion | flops 18874368 | bytes 4739584 | tf_op jit(solution)/shard_map/add | solution.py:93
  58.5 5.2 %reshape.308 = f32[1024,3,2,128]{3,2,1,0:T(2,128)} reshape(f32[1024,768]{1,0:T(8,128)} %select_add_fusion) | data formatting | bytes 6291456 | tf_op jit(solution)/shard_map/reshape | solution.py:94
  63.7 1.6 slice.86
  65.3 1.7 fusion.85
  68.4 0.7 fusion.24
  69.8 3.4 collective-permute-start.5
  73.2 2.4 collective-permute-start.6
  75.7 0.6 subtract_bitcast_fusion
  76.4 0.7 fusion.18
  77.1 3.6 %collective-permute-start.1 = (bf16[2,256,256]{1,2,0:T(8,128)(2,1)}, bf16[2,256,256]{1,2,0:T(8,128)(2,1)S(1)}, u32[]{:S(2)}, u32[]{:S(2)}) collective-permute-start(bf16[2,256,256]{1,2,0:T(8,128)(2,1)} %fusion.18), channel_id=1, source_target_pairs={{0,4},{4,8},{8,12},{12,16},{16,20},{20,24},{24,28},{28,32},{32,36}... | collective-permute-start | bytes 786440 | tf_op jit(solution)/shard_map/ppermute | solution.py:17
  80.7 3.0 fusion.3
  83.8 3.0 fusion.1
  86.7 4.5 %fusion.12 = f32[512,2,128]{0,2,1:T(8,128)S(1)} fusion(f32[2,512,1040]{1,2,0:T(8,128)} %fusion.3, bf16[1024,2,128]{2,0,1:T(8,128)(2,1)} %bitcast.89, bf16[16,2,128]{2,0,1:T(8,128)(2,1)S(1)} %copy.81), kind=kOutput, calls=%fused_computation.29 | convolution fusion | flops 275826688 | bytes 5316608 | tf_op jit(solution)/shard_map/hqk,khd->qhd/dot_general | solution.py:145
  91.3 1.5 subtract_convert_fusion.3
  92.7 3.6 collective-permute-start.8
  96.3 6.0 %collective-permute-start.7 = (bf16[2,256,128]{1,2,0:T(8,128)(2,1)S(1)}, bf16[2,256,128]{1,2,0:T(8,128)(2,1)S(1)}, u32[]{:S(2)}, u32[]{:S(2)}) collective-permute-start(bf16[2,256,128]{1,2,0:T(8,128)(2,1)S(1)} %get-tuple-element.18), channel_id=1, source_target_pairs={{0,8},{4,12},{8,16},{12,20},{16,24},{20,28},{24,32},{28,36},{32,40... | collective-permute-start | bytes 393224 | tf_op jit(solution)/shard_map/ppermute | solution.py:17
  102.3 0.6 fusion.87
  102.9 1.9 collective-permute-start.2
  104.9 0.7 subtract_convert_fusion.2
  105.6 3.7 %collective-permute-start.10 = (bf16[2,256,128]{1,2,0:T(8,128)(2,1)S(1)}, bf16[2,256,128]{1,2,0:T(8,128)(2,1)S(1)}, u32[]{:S(2)}, u32[]{:S(2)}) collective-permute-start(bf16[2,256,128]{1,2,0:T(8,128)(2,1)S(1)} %get-tuple-element.15), channel_id=1, source_target_pairs={{0,16},{4,20},{8,24},{12,28},{16,32},{20,36},{24,40},{28,44},{32,4... | collective-permute-start | bytes 393224 | tf_op jit(solution)/shard_map/ppermute | solution.py:17
  109.2 4.8 %collective-permute-start.9 = (bf16[2,256,128]{1,2,0:T(8,128)(2,1)S(1)}, bf16[2,256,128]{1,2,0:T(8,128)(2,1)S(1)}, u32[]{:S(2)}, u32[]{:S(2)}) collective-permute-start(bf16[2,256,128]{1,2,0:T(8,128)(2,1)S(1)} %get-tuple-element.16), channel_id=1, source_target_pairs={{0,16},{4,20},{8,24},{12,28},{16,32},{20,36},{24,40},{28,44},{32,4... | collective-permute-start | bytes 393224 | tf_op jit(solution)/shard_map/ppermute | solution.py:17
  114.4 1.9 collective-permute-start.3
  116.4 1.3 collective-permute-done.9
  117.7 0.7 subtract_convert_fusion.1
  118.4 8.6 %collective-permute-start.12 = (bf16[2,256,128]{1,2,0:T(8,128)(2,1)S(1)}, bf16[2,256,128]{1,2,0:T(8,128)(2,1)S(1)}, u32[]{:S(2)}, u32[]{:S(2)}) collective-permute-start(bf16[2,256,128]{1,2,0:T(8,128)(2,1)S(1)} %get-tuple-element.13), channel_id=1, source_target_pairs={{0,32},{4,36},{8,40},{12,44},{16,48},{20,52},{24,56},{28,60},{32,6... | collective-permute-start | bytes 393224 | tf_op jit(solution)/shard_map/ppermute | solution.py:17
  127.0 5.2 %collective-permute-start.11 = (bf16[2,256,128]{1,2,0:T(8,128)(2,1)S(1)}, bf16[2,256,128]{1,2,0:T(8,128)(2,1)S(1)}, u32[]{:S(2)}, u32[]{:S(2)}) collective-permute-start(bf16[2,256,128]{1,2,0:T(8,128)(2,1)S(1)} %get-tuple-element.14), channel_id=1, source_target_pairs={{0,32},{4,36},{8,40},{12,44},{16,48},{20,52},{24,56},{28,60},{32,6... | collective-permute-start | bytes 393224 | tf_op jit(solution)/shard_map/ppermute | solution.py:17
  132.6 6.9 %collective-permute-start.4 = (bf16[2,256,256]{2,1,0:T(8,128)(2,1)S(1)}, bf16[2,256,256]{2,1,0:T(8,128)(2,1)S(1)}, u32[]{:S(2)}, u32[]{:S(2)}) collective-permute-start(bf16[2,256,256]{2,1,0:T(8,128)(2,1)S(1)} %get-tuple-element.40), channel_id=1, source_target_pairs={{0,32},{4,36},{8,40},{12,44},{16,48},{20,52},{24,56},{28,60},{32,6... | collective-permute-start | bytes 786440 | tf_op jit(solution)/shard_map/ppermute | solution.py:17
  139.5 0.7 subtract_convert_fusion
  140.2 8.9 %collective-permute-start.14 = (bf16[2,256,128]{1,2,0:T(8,128)(2,1)S(1)}, bf16[2,256,128]{1,2,0:T(8,128)(2,1)S(1)}, u32[]{:S(2)}, u32[]{:S(2)}) collective-permute-start(bf16[2,256,128]{1,2,0:T(8,128)(2,1)S(1)} %get-tuple-element.11), channel_id=1, source_target_pairs={{0,64},{4,68},{8,72},{12,76},{16,80},{20,84},{24,88},{28,92},{32,9... | collective-permute-start | bytes 393224 | tf_op jit(solution)/shard_map/ppermute | solution.py:17
  149.1 3.2 collective-permute-start.13
  152.3 2.6 collective-permute-done.4
  155.4 0.7 fusion.26
  156.1 8.8 %collective-permute-start.16 = (bf16[2,128,128]{1,2,0:T(8,128)(2,1)S(1)}, bf16[2,128,128]{1,2,0:T(8,128)(2,1)S(1)}, u32[]{:S(2)}, u32[]{:S(2)}) collective-permute-start(bf16[2,128,128]{1,2,0:T(8,128)(2,1)S(1)} %get-tuple-element.9), channel_id=1, source_target_pairs={{0,4},{4,8},{8,12},{12,16},{16,20},{20,24},{24,28},{28,32},{32,36}... | collective-permute-start | bytes 196616 | tf_op jit(solution)/shard_map/ppermute | solution.py:17
  164.9 1.9 collective-permute-start.15
  166.8 4.5 %fusion.13 = f32[512,2,128]{0,2,1:T(8,128)S(1)} fusion(f32[2,512,1040]{1,2,0:T(8,128)} %fusion.1, bf16[1024,2,128]{2,0,1:T(8,128)(2,1)} %bitcast.90, bf16[16,2,128]{2,0,1:T(8,128)(2,1)S(1)} %copy.81), kind=kOutput, calls=%fused_computation.30 | convolution fusion | flops 275826688 | bytes 5316608 | tf_op jit(solution)/shard_map/hqk,khd->qhd/dot_general | solution.py:145
  172.4 2.1 convolution_convert_fusion
  174.6 54.7 %reduce-scatter.3.cloned.1.call-done = bf16[1024,256]{1,0:T(8,128)(2,1)} async-done(((bf16[1024,1024]{1,0:T(8,128)(2,1)}), bf16[1024,256]{1,0:T(8,128)(2,1)}) %reduce-scatter.3.cloned.1.call-update) | async-done | bytes 524304 | tf_op jit(solution)/shard_map/reduce_scatter | solution.py:150
  229.2 2.0 add_convert_fusion.1
  231.5 50.1 %all-gather.2.cloned.1.call-done = bf16[1024,1024]{1,0:T(8,128)(2,1)} async-done(((bf16[1024,256]{1,0:T(8,128)(2,1)}), bf16[1024,1024]{1,0:T(8,128)(2,1)}) %all-gather.2.cloned.1.call-update) | async-done | bytes 2097168 | tf_op jit(solution)/shard_map/all_gather | solution.py:154
  281.5 2.1 multiply_reduce_fusion
  283.6 4.9 %fusion.91 = f32[1024,704]{0,1:T(8,128)} fusion(bf16[1024,1024]{1,0:T(8,128)(2,1)} %all-gather.2.cloned.1.call-done, bf16[1024,704]{0,1:T(8,128)(2,1)S(1)} %copy-done.19), kind=kOutput, calls=%fused_computation.159 | convolution fusion | flops 1476395008 | bytes 6422528 | tf_op jit(solution)/shard_map/dot_general | solution.py:156
  288.5 7.8 %convolution_convert_fusion.1 = bf16[1024,1024]{1,0:T(8,128)(2,1)} fusion(bf16[704,1024]{1,0:T(8,128)(2,1)S(1)} %copy-done, f32[1024,704]{0,1:T(8,128)} %fusion.91, bf16[1024,1024]{1,0:T(8,128)(2,1)} %all-gather.2.cloned.1.call-done, bf16[1024,704]{0,1:T(8,128)(2,1)} %param.20, f32[1024]{0:T(1024)S(1)} %add_rsqrt_fusion.3), kind=kOutput, calls=%fused_computation.22 | convolution fusion | flops 2959605760 | bytes 9965568 | tf_op jit(solution)/shard_map/dot_general | solution.py:161
  296.3 51.2 %reduce-scatter.5.cloned.1.call-done = bf16[1024,256]{1,0:T(8,128)(2,1)} async-done(((bf16[1024,1024]{1,0:T(8,128)(2,1)}), bf16[1024,256]{1,0:T(8,128)(2,1)}) %reduce-scatter.5.cloned.1.call-update) | async-done | bytes 524304 | tf_op jit(solution)/shard_map/reduce_scatter | solution.py:162
  347.6 2.0 add_convert_fusion
  (93 shorter events, 8.8 us)
Async XLA Ops:
  6.5 282.0 %copy-start = (bf16[704,1024]{1,0:T(8,128)(2,1)S(1)}, bf16[704,1024]{1,0:T(8,128)(2,1)}, u32[]{:S(2)}) copy-start(bf16[704,1024]{1,0:T(8,128)(2,1)} %param.21) | copy-start | bytes 4325380
  7.9 10.7 %copy-start.14 = (bf16[2,16,256]{2,1,0:T(8,128)(2,1)S(1)}, bf16[2,16,256]{2,1,0:T(8,128)(2,1)}, u32[]{:S(2)}) copy-start(bf16[2,16,256]{2,1,0:T(8,128)(2,1)} %param.17) | copy-start | bytes 49156
  9.5 31.0 %all-to-all-start = ((bf16[4,1024,256]{1,2,0:T(8,128)(2,1)}), bf16[4,1024,256]{1,2,0:T(8,128)(2,1)S(1)}, u32[]{:S(2)}, u32[]{:S(2)}) async-start(bf16[4,1024,256]{1,2,0:T(8,128)(2,1)} %stack.2), calls=%async_computation | async-start | bytes 4194304 | tf_op jit(solution)/shard_map/all_to_all | solution.py:79
  14.3 214.9 %reduce-scatter.3.cloned.1.call-start = ((), (), s32[]{:S(2)}) async-start(), calls=%async_computation.3 | async-start | bytes 2621440 | tf_op jit(solution)/shard_map/reduce_scatter | solution.py:150
  27.2 2.9 copy-start.9
  41.0 10.1 %copy-start.13 = (f32[3,256]{1,0:T(4,128)S(1)}, f32[3,256]{1,0:T(4,128)}, u32[]{:S(2)}) copy-start(f32[3,256]{1,0:T(4,128)} %get-tuple-element.7) | copy-start | bytes 9220
  41.0 10.2 %copy-start.12 = (f32[3,256]{1,0:T(4,128)S(1)}, f32[3,256]{1,0:T(4,128)}, u32[]{:S(2)}) copy-start(f32[3,256]{1,0:T(4,128)} %get-tuple-element.8) | copy-start | bytes 9220
  41.0 10.2 %copy-start.11 = (bf16[1,16,256]{2,1,0:T(8,128)(2,1)S(1)}, bf16[1,16,256]{2,1,0:T(8,128)(2,1)}, u32[]{:S(2)}) copy-start(bf16[1,16,256]{2,1,0:T(8,128)(2,1)} %get-tuple-element.27) | copy-start | bytes 24580
  44.4 1.2 copy-start.3
  45.6 5.7 %collective-permute-start = (bf16[3,768]{1,0:T(4,128)(2,1)S(1)}, bf16[3,768]{1,0:T(4,128)(2,1)S(1)}, u32[]{:S(2)}, u32[]{:S(2)}) collective-permute-start(bf16[3,768]{1,0:T(4,128)(2,1)S(1)} %slice.81), channel_id=1, source_target_pairs={{0,4},{4,8},{8,12},{12,16},{16,20},{20,24},{24,28},{28,32},{32,36}... | collective-permute-start | bytes 13832 | tf_op jit(solution)/shard_map/ppermute | solution.py:17
  67.0 0.9 copy-start.17
  67.0 2.7 copy-start.7
  67.4 8.2 %copy-start.10 = (f32[128,128]{0,1:T(8,128)S(1)}, f32[128,128]{0,1:T(8,128)}, u32[]{:S(2)}) copy-start(f32[128,128]{0,1:T(8,128)} %copy-done.9) | copy-start | bytes 196612
  67.4 8.2 %copy-start.16 = (f32[2]{0:T(128)S(1)}, f32[2]{0:T(128)}, u32[]{:S(2)}) copy-start(f32[2]{0:T(128)} %get-tuple-element.19) | copy-start | bytes 28
  67.5 8.2 %copy-start.18 = (f32[2]{0:T(128)S(1)}, f32[2]{0:T(128)}, u32[]{:S(2)}) copy-start(f32[2]{0:T(128)} %get-tuple-element.31) | copy-start | bytes 28
  67.8 8.5 %copy-start.6 = (f32[1,2,128,128]{2,3,1,0:T(8,128)S(1)}, f32[1,2,128,128]{2,3,1,0:T(8,128)}, u32[]{:S(2)}) copy-start(f32[1,2,128,128]{2,3,1,0:T(8,128)} %broadcast_multiply_fusion) | copy-start | bytes 393220
  69.0 11.7 %copy-start.5 = (pred[512,1040]{0,1:T(8,128)(4,1)S(1)}, pred[512,1040]{0,1:T(8,128)(4,1)}, u32[]{:S(2)}) copy-start(pred[512,1040]{0,1:T(8,128)(4,1)} %get-tuple-element.30) | copy-start | bytes 1597444
  69.0 11.7 %copy-start.15 = (bf16[16,2,128]{2,0,1:T(8,128)(2,1)S(1)}, bf16[16,2,128]{2,0,1:T(8,128)(2,1)}, u32[]{:S(2)}) copy-start(bf16[16,2,128]{2,0,1:T(8,128)(2,1)} %fusion.52) | copy-start | bytes 24580
  69.8 21.5 %collective-permute-start.5 = (bf16[2,256,128]{1,2,0:T(8,128)(2,1)}, bf16[2,256,128]{1,2,0:T(8,128)(2,1)}, u32[]{:S(2)}, u32[]{:S(2)}) collective-permute-start(bf16[2,256,128]{1,2,0:T(8,128)(2,1)} %fusion.24), channel_id=1, source_target_pairs={{0,4},{4,8},{8,12},{12,16},{16,20},{20,24},{24,28},{28,32},{32,36}... | collective-permute-start | bytes 393224 | tf_op jit(solution)/shard_map/ppermute | solution.py:17
  73.2 18.0 %collective-permute-start.6 = (bf16[2,256,128]{1,2,0:T(8,128)(2,1)S(1)}, bf16[2,256,128]{1,2,0:T(8,128)(2,1)}, u32[]{:S(2)}, u32[]{:S(2)}) collective-permute-start(bf16[2,256,128]{1,2,0:T(8,128)(2,1)S(1)} %fusion.25), channel_id=1, source_target_pairs={{0,4},{4,8},{8,12},{12,16},{16,20},{20,24},{24,28},{28,32},{32,36}... | collective-permute-start | bytes 393224 | tf_op jit(solution)/shard_map/ppermute | solution.py:17
  77.1 25.2 %collective-permute-start.1 = (bf16[2,256,256]{1,2,0:T(8,128)(2,1)}, bf16[2,256,256]{1,2,0:T(8,128)(2,1)S(1)}, u32[]{:S(2)}, u32[]{:S(2)}) collective-permute-start(bf16[2,256,256]{1,2,0:T(8,128)(2,1)} %fusion.18), channel_id=1, source_target_pairs={{0,4},{4,8},{8,12},{12,16},{16,20},{20,24},{24,28},{28,32},{32,36}... | collective-permute-start | bytes 786440 | tf_op jit(solution)/shard_map/ppermute | solution.py:17
  80.7 3.0 copy-start.4
  92.7 12.1 %collective-permute-start.8 = (bf16[2,256,128]{1,2,0:T(8,128)(2,1)S(1)}, bf16[2,256,128]{1,2,0:T(8,128)(2,1)S(1)}, u32[]{:S(2)}, u32[]{:S(2)}) collective-permute-start(bf16[2,256,128]{1,2,0:T(8,128)(2,1)S(1)} %get-tuple-element.17), channel_id=1, source_target_pairs={{0,8},{4,12},{8,16},{12,20},{16,24},{20,28},{24,32},{28,36},{32,40... | collective-permute-start | bytes 393224 | tf_op jit(solution)/shard_map/ppermute | solution.py:17
  96.3 8.6 %collective-permute-start.7 = (bf16[2,256,128]{1,2,0:T(8,128)(2,1)S(1)}, bf16[2,256,128]{1,2,0:T(8,128)(2,1)S(1)}, u32[]{:S(2)}, u32[]{:S(2)}) collective-permute-start(bf16[2,256,128]{1,2,0:T(8,128)(2,1)S(1)} %get-tuple-element.18), channel_id=1, source_target_pairs={{0,8},{4,12},{8,16},{12,20},{16,24},{20,28},{24,32},{28,36},{32,40... | collective-permute-start | bytes 393224 | tf_op jit(solution)/shard_map/ppermute | solution.py:17
  102.9 11.1 %collective-permute-start.2 = (bf16[2,256,256]{2,1,0:T(8,128)(2,1)S(1)}, bf16[2,256,256]{2,1,0:T(8,128)(2,1)S(1)}, u32[]{:S(2)}, u32[]{:S(2)}) collective-permute-start(bf16[2,256,256]{2,1,0:T(8,128)(2,1)S(1)} %get-tuple-element.34), channel_id=1, source_target_pairs={{0,8},{4,12},{8,16},{12,20},{16,24},{20,28},{24,32},{28,36},{32,40... | collective-permute-start | bytes 786440 | tf_op jit(solution)/shard_map/ppermute | solution.py:17
  105.6 10.8 %collective-permute-start.10 = (bf16[2,256,128]{1,2,0:T(8,128)(2,1)S(1)}, bf16[2,256,128]{1,2,0:T(8,128)(2,1)S(1)}, u32[]{:S(2)}, u32[]{:S(2)}) collective-permute-start(bf16[2,256,128]{1,2,0:T(8,128)(2,1)S(1)} %get-tuple-element.15), channel_id=1, source_target_pairs={{0,16},{4,20},{8,24},{12,28},{16,32},{20,36},{24,40},{28,44},{32,4... | collective-permute-start | bytes 393224 | tf_op jit(solution)/shard_map/ppermute | solution.py:17
  109.2 8.5 %collective-permute-start.9 = (bf16[2,256,128]{1,2,0:T(8,128)(2,1)S(1)}, bf16[2,256,128]{1,2,0:T(8,128)(2,1)S(1)}, u32[]{:S(2)}, u32[]{:S(2)}) collective-permute-start(bf16[2,256,128]{1,2,0:T(8,128)(2,1)S(1)} %get-tuple-element.16), channel_id=1, source_target_pairs={{0,16},{4,20},{8,24},{12,28},{16,32},{20,36},{24,40},{28,44},{32,4... | collective-permute-start | bytes 393224 | tf_op jit(solution)/shard_map/ppermute | solution.py:17
  114.4 17.7 %collective-permute-start.3 = (bf16[2,256,256]{2,1,0:T(8,128)(2,1)S(1)}, bf16[2,256,256]{2,1,0:T(8,128)(2,1)S(1)}, u32[]{:S(2)}, u32[]{:S(2)}) collective-permute-start(bf16[2,256,256]{2,1,0:T(8,128)(2,1)S(1)} %get-tuple-element.37), channel_id=1, source_target_pairs={{0,16},{4,20},{8,24},{12,28},{16,32},{20,36},{24,40},{28,44},{32,4... | collective-permute-start | bytes 786440 | tf_op jit(solution)/shard_map/ppermute | solution.py:17
  118.4 21.1 %collective-permute-start.12 = (bf16[2,256,128]{1,2,0:T(8,128)(2,1)S(1)}, bf16[2,256,128]{1,2,0:T(8,128)(2,1)S(1)}, u32[]{:S(2)}, u32[]{:S(2)}) collective-permute-start(bf16[2,256,128]{1,2,0:T(8,128)(2,1)S(1)} %get-tuple-element.13), channel_id=1, source_target_pairs={{0,32},{4,36},{8,40},{12,44},{16,48},{20,52},{24,56},{28,60},{32,6... | collective-permute-start | bytes 393224 | tf_op jit(solution)/shard_map/ppermute | solution.py:17
  127.0 12.5 %collective-permute-start.11 = (bf16[2,256,128]{1,2,0:T(8,128)(2,1)S(1)}, bf16[2,256,128]{1,2,0:T(8,128)(2,1)S(1)}, u32[]{:S(2)}, u32[]{:S(2)}) collective-permute-start(bf16[2,256,128]{1,2,0:T(8,128)(2,1)S(1)} %get-tuple-element.14), channel_id=1, source_target_pairs={{0,32},{4,36},{8,40},{12,44},{16,48},{20,52},{24,56},{28,60},{32,6... | collective-permute-start | bytes 393224 | tf_op jit(solution)/shard_map/ppermute | solution.py:17
  132.6 22.4 %collective-permute-start.4 = (bf16[2,256,256]{2,1,0:T(8,128)(2,1)S(1)}, bf16[2,256,256]{2,1,0:T(8,128)(2,1)S(1)}, u32[]{:S(2)}, u32[]{:S(2)}) collective-permute-start(bf16[2,256,256]{2,1,0:T(8,128)(2,1)S(1)} %get-tuple-element.40), channel_id=1, source_target_pairs={{0,32},{4,36},{8,40},{12,44},{16,48},{20,52},{24,56},{28,60},{32,6... | collective-permute-start | bytes 786440 | tf_op jit(solution)/shard_map/ppermute | solution.py:17
  140.2 15.1 %collective-permute-start.14 = (bf16[2,256,128]{1,2,0:T(8,128)(2,1)S(1)}, bf16[2,256,128]{1,2,0:T(8,128)(2,1)S(1)}, u32[]{:S(2)}, u32[]{:S(2)}) collective-permute-start(bf16[2,256,128]{1,2,0:T(8,128)(2,1)S(1)} %get-tuple-element.11), channel_id=1, source_target_pairs={{0,64},{4,68},{8,72},{12,76},{16,80},{20,84},{24,88},{28,92},{32,9... | collective-permute-start | bytes 393224 | tf_op jit(solution)/shard_map/ppermute | solution.py:17
  149.1 6.2 %collective-permute-start.13 = (bf16[2,256,128]{1,2,0:T(8,128)(2,1)S(1)}, bf16[2,256,128]{1,2,0:T(8,128)(2,1)S(1)}, u32[]{:S(2)}, u32[]{:S(2)}) collective-permute-start(bf16[2,256,128]{1,2,0:T(8,128)(2,1)S(1)} %get-tuple-element.12), channel_id=1, source_target_pairs={{0,64},{4,68},{8,72},{12,76},{16,80},{20,84},{24,88},{28,92},{32,9... | collective-permute-start | bytes 393224 | tf_op jit(solution)/shard_map/ppermute | solution.py:17
  156.1 15.3 %collective-permute-start.16 = (bf16[2,128,128]{1,2,0:T(8,128)(2,1)S(1)}, bf16[2,128,128]{1,2,0:T(8,128)(2,1)S(1)}, u32[]{:S(2)}, u32[]{:S(2)}) collective-permute-start(bf16[2,128,128]{1,2,0:T(8,128)(2,1)S(1)} %get-tuple-element.9), channel_id=1, source_target_pairs={{0,4},{4,8},{8,12},{12,16},{16,20},{20,24},{24,28},{28,32},{32,36}... | collective-permute-start | bytes 196616 | tf_op jit(solution)/shard_map/ppermute | solution.py:17
  164.9 6.5 %collective-permute-start.15 = (bf16[2,128,128]{1,2,0:T(8,128)(2,1)S(1)}, bf16[2,128,128]{1,2,0:T(8,128)(2,1)S(1)}, u32[]{:S(2)}, u32[]{:S(2)}) collective-permute-start(bf16[2,128,128]{1,2,0:T(8,128)(2,1)S(1)} %get-tuple-element.10), channel_id=1, source_target_pairs={{0,4},{4,8},{8,12},{12,16},{16,20},{20,24},{24,28},{28,32},{32,36}... | collective-permute-start | bytes 196616 | tf_op jit(solution)/shard_map/ppermute | solution.py:17
  171.4 1.0 copy-start.8
  172.3 57.0 %copy-start.2 = (bf16[1024,256]{1,0:T(8,128)(2,1)S(1)}, bf16[1024,256]{1,0:T(8,128)(2,1)}, u32[]{:S(2)}) copy-start(bf16[1024,256]{1,0:T(8,128)(2,1)} %param.11) | copy-start | bytes 1572868
  174.5 109.1 %copy-start.19 = (bf16[1024,704]{0,1:T(8,128)(2,1)S(1)}, bf16[1024,704]{0,1:T(8,128)(2,1)}, u32[]{:S(2)}) copy-start(bf16[1024,704]{0,1:T(8,128)(2,1)} %param.19) | copy-start | bytes 4325380
  174.5 107.0 %all-gather.2.cloned.1.call-start = ((), (), s32[]{:S(2)}) async-start(), calls=%async_computation.4 | async-start | bytes 2621440 | tf_op jit(solution)/shard_map/all_gather | solution.py:154
  231.2 116.4 %reduce-scatter.5.cloned.1.call-start = ((), (), s32[]{:S(2)}) async-start(), calls=%async_computation.5 | async-start | bytes 2621440 | tf_op jit(solution)/shard_map/reduce_scatter | solution.py:162
  288.5 59.1 %copy-start.1 = (bf16[1024,256]{1,0:T(8,128)(2,1)S(1)}, bf16[1024,256]{1,0:T(8,128)(2,1)}, u32[]{:S(2)}) copy-start(bf16[1024,256]{1,0:T(8,128)(2,1)} %add_convert_fusion.1) | copy-start | bytes 1572868
Sparse Core Ops, SparseCore 0:
  174.6 54.5 reduce-scatter.2
  231.3 50.1 all-gather.1
  296.5 51.0 reduce-scatter.4
